TPU v7x, 32 devices: a whole 2x2x4 slice. The times are simulated.
32 devices in a mesh: ctx: 8 (over z, y), tp: 4 (over x, core).
Axes of the slice: x: 2, y: 2, z: 4, core: 2. Of those that a mesh axis runs over, the one named last changes fastest.
Arguments:
- tokens: bfloat16 [1024, 4096], P('ctx'), may hold values from -6 to 6
- w_query: bfloat16 [4096, 2048], P('ctx', 'tp'), may hold values from -0.09375 to 0.09375
- w_key: bfloat16 [4096, 2048], P('ctx', 'tp'), may hold values from -0.09375 to 0.09375
- w_value: bfloat16 [4096, 2048], P('ctx', 'tp'), may hold values from -0.09375 to 0.09375
- taps_query: float32 [3, 2048], P(None, 'tp'), may hold values from -3.5 to 3.5
- taps_key: float32 [3, 2048], P(None, 'tp'), may hold values from -3.5 to 3.5
- taps_value: float32 [3, 2048], P(None, 'tp'), may hold values from -3.5 to 3.5
- decay_rate: float32 [16, 2048], P(None, 'tp'), may hold values from 1e-05 to 0.03
- residue: float32 [16, 2048], P(None, 'tp'), may hold values from -1.5 to 1.5
- skip_gain: float32 [2048], P('tp'), may hold values from -3 to 3
- w_out: bfloat16 [2048, 4096], P('ctx', 'tp'), may hold values from -0.125 to 0.125
Outputs:
- layer_out: bfloat16 [1024, 4096], P('ctx', 'tp')
All inputs are finite; a program needn't handle non-finite values.
Results may differ from a plain program's by a relative error of at most 0.015.
Values may be sent and summed in bfloat16 or wider, within the bound.
No kernel may reach another device: no remote copies, remote signals or barrier semaphores. Data moves between devices by JAX's collectives and lax.ppermute only.
A program may use at most 128 MiB of HBM per device.

v0:
```python
import math
import jax
import jax.numpy as jnp
from jax import lax
from jax.sharding import PartitionSpec as P


def exact_mul(left, right):
    return jnp.matmul(left, right, precision=lax.Precision.HIGHEST)


def dft_tables(count):
    index = jnp.arange(count, dtype=jnp.int32)
    angle = (index[:, None] * index[None, :] % count).astype(jnp.float32) * (2.0 * math.pi / count)
    return (jnp.cos(angle), jnp.sin(angle))


def long_conv(signal, rates, residues, skips, rows_a, cols_b):
    half = rows_a // 2
    total_len = rows_a * cols_b
    length = half * cols_b
    cos_a, sin_a = dft_tables(rows_a)
    cos_b, sin_b = dft_tables(cols_b)
    index_a = jnp.arange(rows_a, dtype=jnp.int32)
    index_b = jnp.arange(cols_b, dtype=jnp.int32)
    twist = (index_a[:, None] * index_b[None, :] % total_len).astype(jnp.float32) * (
        2.0 * math.pi / total_len
    )
    twist_cos = jnp.cos(twist)
    twist_sin = jnp.sin(twist)
    times = jnp.arange(length, dtype=jnp.float32)

    def one_channel(items):
        channel, rate, weight, skip = items
        channel_f = channel.astype(jnp.float32)
        coefs = weight * jnp.sqrt(2.0 * rate)
        kernel = jnp.sum(coefs[:, None] * jnp.exp(-rate[:, None] * times[None, :]), axis=0)
        stacked = jnp.stack([channel_f, kernel]).reshape(2, half, cols_b)
        first_re = exact_mul(cos_a[:, :half], stacked)
        first_im = -exact_mul(sin_a[:, :half], stacked)
        turned_re = first_re * twist_cos + first_im * twist_sin
        turned_im = first_im * twist_cos - first_re * twist_sin
        spec_re = exact_mul(turned_re, cos_b) + exact_mul(turned_im, sin_b)
        spec_im = exact_mul(turned_im, cos_b) - exact_mul(turned_re, sin_b)
        prod_re = spec_re[0] * spec_re[1] - spec_im[0] * spec_im[1]
        prod_im = spec_re[0] * spec_im[1] + spec_im[0] * spec_re[1]
        back_re = exact_mul(prod_re, cos_b) - exact_mul(prod_im, sin_b)
        back_im = exact_mul(prod_im, cos_b) + exact_mul(prod_re, sin_b)
        unturned_re = back_re * twist_cos - back_im * twist_sin
        unturned_im = back_im * twist_cos + back_re * twist_sin
        result = (
            exact_mul(cos_a[:half], unturned_re) - exact_mul(sin_a[:half], unturned_im)
        ) / total_len
        return result.reshape(length) + skip * channel_f

    return lax.map(one_channel, (signal, rates, residues, skips))


def body(
    tokens,
    w_query,
    w_key,
    w_value,
    taps_query,
    taps_key,
    taps_value,
    decay_rate,
    residue,
    skip_gain,
    w_out,
):
    tok_count = tokens.shape[0]
    width_part = w_query.shape[1]

    def add_rows(piece):
        return jnp.dot(tokens, piece, preferred_element_type=jnp.float32)

    queries = add_rows(lax.all_gather(w_query, "ctx", axis=0, tiled=True))
    keys_proj = add_rows(lax.all_gather(w_key, "ctx", axis=0, tiled=True))
    values_proj = add_rows(lax.all_gather(w_value, "ctx", axis=0, tiled=True))
    queries = queries.astype(jnp.bfloat16)
    keys_proj = keys_proj.astype(jnp.bfloat16)
    values_proj = values_proj.astype(jnp.bfloat16)
    ctx_count = lax.axis_size("ctx")
    chan_count = width_part // ctx_count
    first = lax.axis_index("ctx") * chan_count
    rates = lax.dynamic_slice_in_dim(decay_rate, first, chan_count, 1).T
    residues = lax.dynamic_slice_in_dim(residue, first, chan_count, 1).T
    skips = lax.dynamic_slice_in_dim(skip_gain, first, chan_count, 0)
    query_chan, key_chan, value_chan = (
        lax.all_to_all(queries.T, "ctx", split_axis=0, concat_axis=1, tiled=True),
        lax.all_to_all(keys_proj.T, "ctx", split_axis=0, concat_axis=1, tiled=True),
        lax.all_to_all(values_proj.T, "ctx", split_axis=0, concat_axis=1, tiled=True),
    )

    def conv_channels(signal_in, taps):
        taps_part = lax.dynamic_slice_in_dim(taps, first, chan_count, 1)
        padded = jnp.pad(signal_in.astype(jnp.float32), ((0, 0), (2, 0)))
        return (
            taps_part[0][:, None] * padded[:, 2:]
            + taps_part[1][:, None] * padded[:, 1:-1]
            + taps_part[2][:, None] * padded[:, :-2]
        )

    gate_channels = conv_channels(query_chan, taps_query).astype(jnp.bfloat16)
    signal = (conv_channels(key_chan, taps_key) * conv_channels(value_chan, taps_value)).astype(
        jnp.bfloat16
    )
    mixed_long = long_conv(signal, rates, residues, skips, tok_count, 2 * ctx_count).astype(
        jnp.bfloat16
    )
    outgoing = (gate_channels.astype(jnp.float32) * mixed_long.astype(jnp.float32)).astype(
        jnp.bfloat16
    )
    gated = lax.all_to_all(outgoing, "ctx", split_axis=1, concat_axis=0, tiled=True).T
    features = lax.all_gather(gated, "tp", axis=1, tiled=True)
    result = jnp.dot(
        features,
        lax.all_gather(w_out, "ctx", axis=0, tiled=True),
        preferred_element_type=jnp.float32,
    )
    return result.astype(jnp.bfloat16)


def solution(mesh):
    in_specs = (
        P("ctx", None),
        P("ctx", "tp"),
        P("ctx", "tp"),
        P("ctx", "tp"),
        P(None, "tp"),
        P(None, "tp"),
        P(None, "tp"),
        P(None, "tp"),
        P(None, "tp"),
        P("tp"),
        P("ctx", "tp"),
    )
    out_specs = P("ctx", "tp")
    return jax.shard_map(body, mesh=mesh, in_specs=in_specs, out_specs=out_specs, check_vma=False)
```

profile of v0, /device:TPU:0, one launch (start us, length us, event | category | flops | bytes accessed | tf_op | source)
XLA Modules:
  0.0 559.2 jit_solution(9386341728542071466)
XLA Ops:
  6.5 0.7 all-gather.9.cloned.1.call-update
  7.3 0.7 all-gather.7.cloned.1.call-update
  8.1 0.7 all-gather.5.cloned.1.call-update
  9.6 0.8 constant_dynamic-slice_fusion.4
  10.4 0.8 constant_dynamic-slice_fusion.2
  11.4 0.8 dynamic_slice.38
  12.1 0.8 constant_dynamic-slice_fusion.6
  12.9 72.7 %all-gather.9.cloned.1.call-done = bf16[4096,512]{1,0:T(8,128)(2,1)} async-done(((bf16[512,512]{1,0:T(8,128)(2,1)}), bf16[4096,512]{1,0:T(8,128)(2,1)}) %all-gather.9.cloned.1.call-update) | async-done | bytes 4194320 | tf_op jit(solution)/shard_map/all_gather | solution.py:80
  85.6 4.1 convolution_convert_fusion.1
  89.8 3.4 all-to-all-start.2
  93.1 67.3 %all-gather.7.cloned.1.call-done = bf16[4096,512]{1,0:T(8,128)(2,1)} async-done(((bf16[512,512]{1,0:T(8,128)(2,1)}), bf16[4096,512]{1,0:T(8,128)(2,1)}) %all-gather.7.cloned.1.call-update) | async-done | bytes 4194320 | tf_op jit(solution)/shard_map/all_gather | solution.py:79
  160.5 4.1 convolution_convert_fusion.2
  164.6 69.7 %all-gather.5.cloned.1.call-done = bf16[4096,512]{1,0:T(8,128)(2,1)} async-done(((bf16[512,512]{1,0:T(8,128)(2,1)}), bf16[4096,512]{1,0:T(8,128)(2,1)}) %all-gather.5.cloned.1.call-update) | async-done | bytes 4194320 | tf_op jit(solution)/shard_map/all_gather | solution.py:78
  234.3 4.1 convolution_convert_fusion.3
  238.4 3.4 all-to-all-start.1
  241.8 9.0 %all-to-all-done.1 = bf16[8,64,128]{2,1,0:T(8,128)(2,1)S(1)} async-done(((bf16[8,64,128]{2,1,0:T(8,128)(2,1)}), bf16[8,64,128]{2,1,0:T(8,128)(2,1)S(1)}, u32[]{:S(2)}, u32[]{:S(2)}) %all-to-all-start.1) | async-done | bytes 131104 | tf_op jit(solution)/shard_map/all_to_all | solution.py:92
  250.9 4.1 all-to-all-start
  255.4 273.1 %while.12 = (s32[]{:T(128)}, bf16[64,1024]{1,0:T(8,128)(2,1)S(1)}, bf16[64,1024]{1,0:T(8,128)(2,1)S(1)}, f32[64,16]{1,0:T(8,128)S(1)}, f32[64,16]{1,0:T(8,128)S(...) while((s32[]{:T(128)}, bf16[64,1024]{1,0:T(8,128)(2,1)S(1)}, ...), condition=%wide.region_2.3_spmd.clone.clone, body=%wide.region_0.2_spmd.clone.clone.sunk | while | flops 14420018 | bytes 821765 | solution.py:56
  258.5 0.6 dynamic_slice.73
  262.7 0.6 dynamic_slice.73
  267.0 0.6 dynamic_slice.73
  275.5 0.6 dynamic_slice.73
  279.8 0.6 dynamic_slice.73
  284.1 0.6 dynamic_slice.73
  288.3 0.6 dynamic_slice.73
  292.6 0.6 dynamic_slice.73
  296.9 0.6 dynamic_slice.73
  301.1 0.6 dynamic_slice.73
  305.4 0.6 dynamic_slice.73
  309.7 0.6 dynamic_slice.73
  313.9 0.6 dynamic_slice.73
  318.2 0.6 dynamic_slice.73
  322.5 0.6 dynamic_slice.73
  326.7 0.6 dynamic_slice.73
  331.0 0.6 dynamic_slice.73
  335.3 0.6 dynamic_slice.73
  339.5 0.6 dynamic_slice.73
  343.8 0.6 dynamic_slice.73
  348.1 0.6 dynamic_slice.73
  352.3 0.6 dynamic_slice.73
  356.6 0.6 dynamic_slice.73
  360.9 0.6 dynamic_slice.73
  365.1 0.6 dynamic_slice.73
  369.4 0.6 dynamic_slice.73
  373.7 0.6 dynamic_slice.73
  377.9 0.6 dynamic_slice.73
  382.2 0.6 dynamic_slice.73
  386.5 0.6 dynamic_slice.73
  390.7 0.6 dynamic_slice.73
  395.0 0.6 dynamic_slice.73
  399.3 0.6 dynamic_slice.73
  403.5 0.6 dynamic_slice.73
  416.3 0.6 dynamic_slice.73
  429.1 0.6 dynamic_slice.73
  441.9 0.6 dynamic_slice.73
  454.7 0.6 dynamic_slice.73
  467.5 0.6 dynamic_slice.73
  480.3 0.6 dynamic_slice.73
  493.1 0.6 dynamic_slice.73
  505.9 0.6 dynamic_slice.73
  518.7 0.6 dynamic_slice.73
  528.8 13.1 %all_to_all.58 = bf16[64,8,128]{2,0,1:T(8,128)(2,1)S(1)} all-to-all(bf16[64,8,128]{2,0,1:T(8,128)(2,1)S(1)} %copy_bitcast_fusion.3), channel_id=1, replica_groups=mesh['ctx'=8,'tp'=4] {'ctx'}, dimensions={1} | all-to-all | bytes 262144 | tf_op jit(solution)/shard_map/all_to_all | solution.py:115
  541.9 7.1 %all_gather.18 = bf16[128,2048]{0,1:T(8,128)(2,1)S(1)} all-gather(bf16[128,512]{0,1:T(8,128)(2,1)S(1)} %bitcast.126), channel_id=1, replica_groups=mesh['ctx'=8,'tp'=4] {'tp'}, dimensions={1}, use_global_device_ids=true | all-gather | bytes 655360 | tf_op jit(solution)/shard_map/all_gather | solution.py:116
  549.1 3.6 convolution_convert_fusion
  (1643 shorter events, 242.0 us)
Async XLA Ops:
  6.5 79.1 %copy-start = (bf16[128,4096]{1,0:T(8,128)(2,1)S(1)}, bf16[128,4096]{1,0:T(8,128)(2,1)}, u32[]{:S(2)}) copy-start(bf16[128,4096]{1,0:T(8,128)(2,1)} %param.13) | copy-start | bytes 3145732
  6.5 79.1 %all-gather.9.cloned.1.call-start = ((), (), s32[]{:S(2)}) async-start(), calls=%async_computation.6 | async-start | bytes 4718592 | tf_op jit(solution)/shard_map/all_gather | solution.py:80
  7.3 153.2 %all-gather.7.cloned.1.call-start = ((), (), s32[]{:S(2)}) async-start(), calls=%async_computation.5 | async-start | bytes 4718592 | tf_op jit(solution)/shard_map/all_gather | solution.py:79
  8.0 226.3 %all-gather.5.cloned.1.call-start = ((), (), s32[]{:S(2)}) async-start(), calls=%async_computation.4 | async-start | bytes 4718592 | tf_op jit(solution)/shard_map/all_gather | solution.py:78
  8.7 540.3 %all-gather.11.cloned.1.call-start = ((), (), s32[]{:S(2)}) async-start(), calls=%async_computation.7 | async-start | bytes 4718592 | tf_op jit(solution)/shard_map/all_gather | solution.py:119
  89.8 148.7 %all-to-all-start.2 = ((bf16[8,64,128]{2,1,0:T(8,128)(2,1)}), bf16[8,64,128]{2,1,0:T(8,128)(2,1)S(1)}, u32[]{:S(2)}, u32[]{:S(2)}) async-start(bf16[8,64,128]{2,1,0:T(8,128)(2,1)} %bitcast.11), calls=%async_computation.2 | async-start | bytes 262144 | tf_op jit(solution)/shard_map/all_to_all | solution.py:93
  238.4 12.4 %all-to-all-start.1 = ((bf16[8,64,128]{2,1,0:T(8,128)(2,1)}), bf16[8,64,128]{2,1,0:T(8,128)(2,1)S(1)}, u32[]{:S(2)}, u32[]{:S(2)}) async-start(bf16[8,64,128]{2,1,0:T(8,128)(2,1)} %bitcast.6), calls=%async_computation.1 | async-start | bytes 262144 | tf_op jit(solution)/shard_map/all_to_all | solution.py:92
  250.9 277.6 %all-to-all-start = ((bf16[8,64,128]{2,1,0:T(8,128)(2,1)}), bf16[8,64,128]{2,1,0:T(8,128)(2,1)S(1)}, u32[]{:S(2)}, u32[]{:S(2)}) async-start(bf16[8,64,128]{2,1,0:T(8,128)(2,1)} %bitcast.1), calls=%async_computation | async-start | bytes 262144 | tf_op jit(solution)/shard_map/all_to_all | solution.py:91
Sparse Core Ops, SparseCore 0:
  9.5 76.0 all-gather.8
  87.7 72.6 all-gather.6
  162.6 71.6 all-gather.4
  236.3 75.7 all-gather.10
where the time goes:
time: 561 us; the launch traced here: 559 us
  waiting for transfers between devices  221 us (39%)
  matrix products  160 us (29%)
  local copies, waits for them, and re-layouts  74.8 us (13%)
  other arithmetic  51.3 us (9%)
  blocking collectives  20.3 us (4%)
  between operations  13.2 us (2%)
  starting transfers between devices  11 us (2%)
  loops' own time  7.56 us (1%)
    dot_general x768, matrix products, exact_mul(): return jnp.matmul(left, right, precision=lax.Precision.HIGHEST)  144 us
    all_gather x1, waiting for transfers between devices, body(): values_proj = add_rows(lax.all_gather(w_value, 'ctx', axis=0, tiled=True))  72.7 us
    all_gather x1, waiting for transfers between devices, body(): queries = add_rows(lax.all_gather(w_query, 'ctx', axis=0, tiled=True))  69.7 us
    all_gather x1, waiting for transfers between devices, body(): keys_proj = add_rows(lax.all_gather(w_key, 'ctx', axis=0, tiled=True))  67.3 us
    dynamic_slice x64, local copies, waits for them, and re-layouts, long_conv(): return lax.map(one_channel, (signal, rates, residues, skips))  37.7 us
    add x64, other arithmetic, one_channel(): return result.reshape(length) + skip * channel_f  36.7 us
    another operation x256, local copies, waits for them, and re-layouts, one_channel(): stacked = jnp.stack([channel_f, kernel]).reshape(2, half, cols_b)  17.5 us
    all_to_all x1, blocking collectives, body(): lax.all_to_all(outgoing, 'ctx', split_axis=1, concat_axis=0, tiled=True)  13.1 us
  transfers between devices with their start and end apart: 7, of which 4 were waited for; matrix products, arithmetic and copies ran while one was open for 50% of the time, Pallas kernels for 0%

commit v1 on v0

--- a/solution.py
+++ b/solution.py
@@ -3,6 +3,28 @@
 import jax.numpy as jnp
 from jax import lax
 from jax.sharding import PartitionSpec as P
+
+
+def apply_the_cards(message, link_axis):
+    found_now = lax.psum(1, axis_name=link_axis)
+    e_next, y, right_arr = (found_now, lax.axis_index(link_axis), message.shape[0])
+    arrivals = tuple(((dev_i, (dev_i + 1) % e_next) for dev_i in range(e_next)))
+    leaves = tuple(((dev_i, (dev_i - 1) % e_next) for dev_i in range(e_next)))
+    a_next = jnp.zeros((*message.shape[:0], e_next * right_arr, *message.shape[1:]), message.dtype)
+    a_next = lax.dynamic_update_slice_in_dim(a_next, message, y * right_arr, axis=0)
+    val2 = carry_out = message
+    out_arr = e_next // 2
+    for to_i in range(1, out_arr + 1):
+        val2 = lax.ppermute(val2, axis_name=link_axis, perm=arrivals)
+        a_next = lax.dynamic_update_slice_in_dim(
+            a_next, val2, (y - to_i) % e_next * right_arr, axis=0
+        )
+        if to_i < e_next - out_arr:
+            carry_out = lax.ppermute(carry_out, axis_name=link_axis, perm=leaves)
+            a_next = lax.dynamic_update_slice_in_dim(
+                a_next, carry_out, (y + to_i) % e_next * right_arr, axis=0
+            )
+    return a_next
 
 
 def exact_mul(left, right):
@@ -75,7 +97,7 @@
     def add_rows(piece):
         return jnp.dot(tokens, piece, preferred_element_type=jnp.float32)
 
-    queries = add_rows(lax.all_gather(w_query, "ctx", axis=0, tiled=True))
+    queries = add_rows(apply_the_cards(w_query, link_axis="ctx"))
     keys_proj = add_rows(lax.all_gather(w_key, "ctx", axis=0, tiled=True))
     values_proj = add_rows(lax.all_gather(w_value, "ctx", axis=0, tiled=True))
     queries = queries.astype(jnp.bfloat16)

time: 561 us -> 542 us (0.966)
  waiting for transfers between devices: 221 us -> 176 us
  starting transfers between devices: 11 us -> 32.3 us
    ppermute x0 -> x7, waiting for transfers between devices: none -> 89.9 us  [the longest x4 87 us: apply_the_cards(): val2 = lax.ppermute(val2, axis_name=link_axis, perm=arrivals)]
    all_gather x1, waiting for transfers between devices: 72.7 us -> 1.01 us  [body(): values_proj = add_rows(lax.all_gather(w_value, 'ctx', axis=0, tiled=True))]
    all_gather x1 -> x0, waiting for transfers between devices: 69.7 us -> none  [body(): queries = add_rows(lax.all_gather(w_query, 'ctx', axis=0, tiled=True))]
    ppermute x0 -> x7, starting transfers between devices: none -> 19 us  [the longest x4 11 us: apply_the_cards(): val2 = lax.ppermute(val2, axis_name=link_axis, perm=arrivals)]
    all_to_all x1, waiting for transfers between devices: 0.01 us -> 7.66 us  [body(): lax.all_to_all(queries.T, 'ctx', split_axis=0, concat_axis=1, tiled=True)]
  transfers between devices with their start and end apart: 7 -> 13, of which waited for: 4 -> 10; matrix products, arithmetic and copies ran while one was open for 50% -> 53% of each run, Pallas kernels for 0% -> 0%
where the time goes in v1:
time: 542 us; the launch traced here: 540 us
  waiting for transfers between devices  176 us (32%)
  matrix products  158 us (29%)
  local copies, waits for them, and re-layouts  77.7 us (14%)
  other arithmetic  56.8 us (10%)
  starting transfers between devices  32.3 us (6%)
  blocking collectives  19 us (4%)
  between operations  13.2 us (2%)
  loops' own time  7.6 us (1%)
    dot_general x768, matrix products, exact_mul(): return jnp.matmul(left, right, precision=lax.Precision.HIGHEST)  144 us
    ppermute x4, waiting for transfers between devices, apply_the_cards(): val2 = lax.ppermute(val2, axis_name=link_axis, perm=arrivals)  87 us
    all_gather x1, waiting for transfers between devices, body(): keys_proj = add_rows(lax.all_gather(w_key, 'ctx', axis=0, tiled=True))  67.5 us
    add x64, other arithmetic, one_channel(): return result.reshape(length) + skip * channel_f  42.2 us
    dynamic_slice x64, local copies, waits for them, and re-layouts, long_conv(): return lax.map(one_channel, (signal, rates, residues, skips))  38 us
    another operation x256, local copies, waits for them, and re-layouts, one_channel(): stacked = jnp.stack([channel_f, kernel]).reshape(2, half, cols_b)  17.5 us
    all_to_all x1, blocking collectives, body(): lax.all_to_all(outgoing, 'ctx', split_axis=1, concat_axis=0, tiled=True)  11.9 us
    ppermute x4, starting transfers between devices, apply_the_cards(): val2 = lax.ppermute(val2, axis_name=link_axis, perm=arrivals)  11 us
  transfers between devices with their start and end apart: 13, of which 10 were waited for; matrix products, arithmetic and copies ran while one was open for 53% of the time, Pallas kernels for 0%

profile of v1, /device:TPU:0, one launch (start us, length us, event | category | flops | bytes accessed | tf_op | source)
XLA Modules:
  0.0 540.3 jit_solution(811241277233286650)
XLA Ops:
  6.5 0.7 all-gather.6.cloned.1.call-update
  7.3 0.7 all-gather.4.cloned.1.call-update
  8.1 3.0 collective-permute-start
  11.1 3.1 collective-permute-start.1
  14.2 25.2 %collective-permute-done = bf16[512,512]{1,0:T(8,128)(2,1)S(1)} collective-permute-done((bf16[512,512]{1,0:T(8,128)(2,1)}, bf16[512,512]{1,0:T(8,128)(2,1)S(1)}, u32[]{:S(2)}, u32[]{:S(2)}) %collective-permute-start) | collective-permute-done | bytes 524320 | tf_op jit(solution)/shard_map/ppermute | solution.py:18
  39.4 2.4 collective-permute-start.2
  41.8 0.8 constant_dynamic-slice_fusion.4
  42.6 3.1 collective-permute-start.3
  46.0 23.9 %collective-permute-done.2 = bf16[512,512]{1,0:T(8,128)(2,1)S(1)} collective-permute-done((bf16[512,512]{1,0:T(8,128)(2,1)S(1)}, bf16[512,512]{1,0:T(8,128)(2,1)S(1)}, u32[]{:S(2)}, u32[]{:S(2)}) %collective-permute-start.2) | collective-permute-done | bytes 524320 | tf_op jit(solution)/shard_map/ppermute | solution.py:18
  69.9 3.0 collective-permute-start.4
  72.9 0.8 constant_dynamic-slice_fusion.2
  74.0 1.4 collective-permute-done.3
  75.4 1.9 collective-permute-start.5
  77.3 28.6 %collective-permute-done.4 = bf16[512,512]{1,0:T(8,128)(2,1)} collective-permute-done((bf16[512,512]{1,0:T(8,128)(2,1)S(1)}, bf16[512,512]{1,0:T(8,128)(2,1)}, u32[]{:S(2)}, u32[]{:S(2)}) %collective-permute-start.4) | collective-permute-done | bytes 524320 | tf_op jit(solution)/shard_map/ppermute | solution.py:18
  105.9 2.6 collective-permute-start.6
  108.6 1.1 constant_dynamic-update-slice_fusion.3
  109.7 1.1 constant_dynamic-update-slice_fusion.2
  110.7 1.5 collective-permute-done.5
  112.3 9.3 %collective-permute-done.6 = bf16[512,512]{1,0:T(8,128)(2,1)S(1)} collective-permute-done((bf16[512,512]{1,0:T(8,128)(2,1)}, bf16[512,512]{1,0:T(8,128)(2,1)S(1)}, u32[]{:S(2)}, u32[]{:S(2)}) %collective-permute-start.6) | collective-permute-done | bytes 524320 | tf_op jit(solution)/shard_map/ppermute | solution.py:18
  121.6 2.0 convolution_convert_fusion.3
  123.6 6.4 %all-to-all-start = ((bf16[8,64,128]{2,1,0:T(8,128)(2,1)}), bf16[8,64,128]{2,1,0:T(8,128)(2,1)S(1)}, u32[]{:S(2)}, u32[]{:S(2)}) async-start(bf16[8,64,128]{2,1,0:T(8,128)(2,1)} %bitcast.1), calls=%async_computation | async-start | bytes 262144 | tf_op jit(solution)/shard_map/all_to_all | solution.py:113
  130.1 0.8 constant_dynamic-slice_fusion.6
  131.0 0.8 dynamic_slice.38
  131.7 7.7 %all-to-all-done = bf16[8,64,128]{2,1,0:T(8,128)(2,1)S(1)} async-done(((bf16[8,64,128]{2,1,0:T(8,128)(2,1)}), bf16[8,64,128]{2,1,0:T(8,128)(2,1)S(1)}, u32[]{:S(2)}, u32[]{:S(2)}) %all-to-all-start) | async-done | bytes 131104 | tf_op jit(solution)/shard_map/all_to_all | solution.py:113
  139.4 1.0 all-gather.6.cloned.1.call-done
  140.4 4.1 convolution_convert_fusion.1
  144.6 3.4 all-to-all-start.2
  148.0 67.5 %all-gather.4.cloned.1.call-done = bf16[4096,512]{1,0:T(8,128)(2,1)} async-done(((bf16[512,512]{1,0:T(8,128)(2,1)}), bf16[4096,512]{1,0:T(8,128)(2,1)}) %all-gather.4.cloned.1.call-update) | async-done | bytes 4194320 | tf_op jit(solution)/shard_map/all_gather | solution.py:101
  215.5 4.1 convolution_convert_fusion.2
  219.6 3.4 all-to-all-start.1
  223.0 8.3 %all-to-all-done.1 = bf16[8,64,128]{2,1,0:T(8,128)(2,1)S(1)} async-done(((bf16[8,64,128]{2,1,0:T(8,128)(2,1)}), bf16[8,64,128]{2,1,0:T(8,128)(2,1)S(1)}, u32[]{:S(2)}, u32[]{:S(2)}) %all-to-all-start.1) | async-done | bytes 131104 | tf_op jit(solution)/shard_map/all_to_all | solution.py:114
  231.8 279.0 %while.12 = (s32[]{:T(128)}, bf16[64,1024]{1,0:T(8,128)(2,1)S(1)}, bf16[64,1024]{1,0:T(8,128)(2,1)S(1)}, f32[64,16]{1,0:T(8,128)S(1)}, f32[64,16]{1,0:T(8,128)S(...) while((s32[]{:T(128)}, bf16[64,1024]{1,0:T(8,128)(2,1)S(1)}, ...), condition=%wide.region_2.3_spmd.clone.clone, body=%wide.region_0.2_spmd.clone.clone.sunk | while | flops 14420018 | bytes 821765 | solution.py:78
  235.5 0.7 multiply_add_fusion.10
  239.8 0.7 multiply_add_fusion.10
  270.3 0.7 multiply_add_fusion.10
  279.1 0.7 multiply_add_fusion.10
  283.4 0.7 multiply_add_fusion.10
  287.8 0.7 multiply_add_fusion.10
  296.5 0.7 multiply_add_fusion.10
  300.9 0.7 multiply_add_fusion.10
  305.2 0.7 multiply_add_fusion.10
  313.9 0.7 multiply_add_fusion.10
  318.3 0.7 multiply_add_fusion.10
  322.7 0.7 multiply_add_fusion.10
  331.4 0.7 multiply_add_fusion.10
  335.7 0.7 multiply_add_fusion.10
  340.1 0.7 multiply_add_fusion.10
  348.8 0.7 multiply_add_fusion.10
  353.2 0.7 multiply_add_fusion.10
  357.5 0.7 multiply_add_fusion.10
  366.3 0.7 multiply_add_fusion.10
  370.6 0.7 multiply_add_fusion.10
  375.0 0.7 multiply_add_fusion.10
  383.7 0.7 multiply_add_fusion.10
  388.1 0.7 multiply_add_fusion.10
  392.4 0.7 multiply_add_fusion.10
  401.1 0.7 multiply_add_fusion.10
  405.5 0.7 multiply_add_fusion.10
  409.9 0.7 multiply_add_fusion.10
  418.6 0.7 multiply_add_fusion.10
  422.9 0.7 multiply_add_fusion.10
  511.1 11.9 %all_to_all.58 = bf16[64,8,128]{2,0,1:T(8,128)(2,1)S(1)} all-to-all(bf16[64,8,128]{2,0,1:T(8,128)(2,1)S(1)} %copy_bitcast_fusion.3), channel_id=1, replica_groups=mesh['ctx'=8,'tp'=4] {'ctx'}, dimensions={1} | all-to-all | bytes 262144 | tf_op jit(solution)/shard_map/all_to_all | solution.py:137
  523.0 7.1 %all_gather.14 = bf16[128,2048]{0,1:T(8,128)(2,1)S(1)} all-gather(bf16[128,512]{0,1:T(8,128)(2,1)S(1)} %bitcast.126), channel_id=1, replica_groups=mesh['ctx'=8,'tp'=4] {'tp'}, dimensions={1}, use_global_device_ids=true | all-gather | bytes 655360 | tf_op jit(solution)/shard_map/all_gather | solution.py:138
  530.2 3.6 convolution_convert_fusion
  (1665 shorter events, 254.1 us)
Async XLA Ops:
  6.5 115.1 %copy-start = (bf16[128,4096]{1,0:T(8,128)(2,1)S(1)}, bf16[128,4096]{1,0:T(8,128)(2,1)}, u32[]{:S(2)}) copy-start(bf16[128,4096]{1,0:T(8,128)(2,1)} %param.13) | copy-start | bytes 3145732
  6.5 67.4 %copy-start.1 = (bf16[512,512]{1,0:T(8,128)(2,1)S(1)}, bf16[512,512]{1,0:T(8,128)(2,1)}, u32[]{:S(2)}) copy-start(bf16[512,512]{1,0:T(8,128)(2,1)} %param.14) | copy-start | bytes 1572868
  6.5 133.9 %all-gather.6.cloned.1.call-start = ((), (), s32[]{:S(2)}) async-start(), calls=%async_computation.5 | async-start | bytes 4718592 | tf_op jit(solution)/shard_map/all_gather | solution.py:102
  7.3 208.2 %all-gather.4.cloned.1.call-start = ((), (), s32[]{:S(2)}) async-start(), calls=%async_computation.4 | async-start | bytes 4718592 | tf_op jit(solution)/shard_map/all_gather | solution.py:101
  8.0 522.1 %all-gather.8.cloned.1.call-start = ((), (), s32[]{:S(2)}) async-start(), calls=%async_computation.6 | async-start | bytes 4718592 | tf_op jit(solution)/shard_map/all_gather | solution.py:141
  8.1 31.4 %collective-permute-start = (bf16[512,512]{1,0:T(8,128)(2,1)}, bf16[512,512]{1,0:T(8,128)(2,1)S(1)}, u32[]{:S(2)}, u32[]{:S(2)}) collective-permute-start(bf16[512,512]{1,0:T(8,128)(2,1)} %param.14), channel_id=1, source_target_pairs={{0,4},{4,8},{8,12},{12,16},{16,20},{20,24},{24,28},{28,0},{1,5},{5... | collective-permute-start | bytes 1572872 | tf_op jit(solution)/shard_map/ppermute | solution.py:18
  11.1 31.5 %collective-permute-start.1 = (bf16[512,512]{1,0:T(8,128)(2,1)}, bf16[512,512]{1,0:T(8,128)(2,1)S(1)}, u32[]{:S(2)}, u32[]{:S(2)}) collective-permute-start(bf16[512,512]{1,0:T(8,128)(2,1)} %param.14), channel_id=1, source_target_pairs={{0,28},{4,0},{8,4},{12,8},{16,12},{20,16},{24,20},{28,24},{1,29},{... | collective-permute-start | bytes 1572872 | tf_op jit(solution)/shard_map/ppermute | solution.py:23
  39.4 30.5 %collective-permute-start.2 = (bf16[512,512]{1,0:T(8,128)(2,1)S(1)}, bf16[512,512]{1,0:T(8,128)(2,1)S(1)}, u32[]{:S(2)}, u32[]{:S(2)}) collective-permute-start(bf16[512,512]{1,0:T(8,128)(2,1)S(1)} %collective-permute-done), channel_id=1, source_target_pairs={{0,4},{4,8},{8,12},{12,16},{16,20},{20,24},{24,28},{28,0},{1,5},{5... | collective-permute-start | bytes 1572872 | tf_op jit(solution)/shard_map/ppermute | solution.py:18
  42.6 32.8 %collective-permute-start.3 = (bf16[512,512]{1,0:T(8,128)(2,1)S(1)}, bf16[512,512]{1,0:T(8,128)(2,1)}, u32[]{:S(2)}, u32[]{:S(2)}) collective-permute-start(bf16[512,512]{1,0:T(8,128)(2,1)S(1)} %collective-permute-done.1), channel_id=1, source_target_pairs={{0,28},{4,0},{8,4},{12,8},{16,12},{20,16},{24,20},{28,24},{1,29},{... | collective-permute-start | bytes 1572872 | tf_op jit(solution)/shard_map/ppermute | solution.py:23
  69.9 36.0 %collective-permute-start.4 = (bf16[512,512]{1,0:T(8,128)(2,1)S(1)}, bf16[512,512]{1,0:T(8,128)(2,1)}, u32[]{:S(2)}, u32[]{:S(2)}) collective-permute-start(bf16[512,512]{1,0:T(8,128)(2,1)S(1)} %collective-permute-done.2), channel_id=1, source_target_pairs={{0,4},{4,8},{8,12},{12,16},{16,20},{20,24},{24,28},{28,0},{1,5},{5... | collective-permute-start | bytes 1572872 | tf_op jit(solution)/shard_map/ppermute | solution.py:18
  75.4 36.8 %collective-permute-start.5 = (bf16[512,512]{1,0:T(8,128)(2,1)}, bf16[512,512]{1,0:T(8,128)(2,1)S(1)}, u32[]{:S(2)}, u32[]{:S(2)}) collective-permute-start(bf16[512,512]{1,0:T(8,128)(2,1)} %collective-permute-done.3), channel_id=1, source_target_pairs={{0,28},{4,0},{8,4},{12,8},{16,12},{20,16},{24,20},{28,24},{1,29},{... | collective-permute-start | bytes 1572872 | tf_op jit(solution)/shard_map/ppermute | solution.py:23
  105.9 15.7 %collective-permute-start.6 = (bf16[512,512]{1,0:T(8,128)(2,1)}, bf16[512,512]{1,0:T(8,128)(2,1)S(1)}, u32[]{:S(2)}, u32[]{:S(2)}) collective-permute-start(bf16[512,512]{1,0:T(8,128)(2,1)} %collective-permute-done.4), channel_id=1, source_target_pairs={{0,4},{4,8},{8,12},{12,16},{16,20},{20,24},{24,28},{28,0},{1,5},{5... | collective-permute-start | bytes 1572872 | tf_op jit(solution)/shard_map/ppermute | solution.py:18
  123.6 15.8 %all-to-all-start = ((bf16[8,64,128]{2,1,0:T(8,128)(2,1)}), bf16[8,64,128]{2,1,0:T(8,128)(2,1)S(1)}, u32[]{:S(2)}, u32[]{:S(2)}) async-start(bf16[8,64,128]{2,1,0:T(8,128)(2,1)} %bitcast.1), calls=%async_computation | async-start | bytes 262144 | tf_op jit(solution)/shard_map/all_to_all | solution.py:113
  144.6 75.0 %all-to-all-start.2 = ((bf16[8,64,128]{2,1,0:T(8,128)(2,1)}), bf16[8,64,128]{2,1,0:T(8,128)(2,1)S(1)}, u32[]{:S(2)}, u32[]{:S(2)}) async-start(bf16[8,64,128]{2,1,0:T(8,128)(2,1)} %bitcast.11), calls=%async_computation.2 | async-start | bytes 262144 | tf_op jit(solution)/shard_map/all_to_all | solution.py:115
  219.6 11.8 %all-to-all-start.1 = ((bf16[8,64,128]{2,1,0:T(8,128)(2,1)}), bf16[8,64,128]{2,1,0:T(8,128)(2,1)S(1)}, u32[]{:S(2)}, u32[]{:S(2)}) async-start(bf16[8,64,128]{2,1,0:T(8,128)(2,1)} %bitcast.6), calls=%async_computation.1 | async-start | bytes 262144 | tf_op jit(solution)/shard_map/all_to_all | solution.py:114
Sparse Core Ops, SparseCore 0:
  9.5 130.8 all-gather.5
  142.6 72.8 all-gather.3
  217.6 73.2 all-gather.7
